TPU v7x, 128 devices: a whole 4x4x4 slice. The times are simulated.
128 devices in a mesh: req: 32 (over x, z, core), mlp: 4 (over y).
Axes of the slice: x: 4, y: 4, z: 4, core: 2. Of those that a mesh axis runs over, the one named last changes fastest.
Arguments:
- hidden_in: bfloat16 [4096, 4096], P('req'), may hold values from -6 to 6
- attn_gain: bfloat16 [4096], replicated, may hold values from 0.5 to 1.5
- w_query: bfloat16 [4096, 2048], P(None, 'mlp'), may hold values from -0.09375 to 0.09375
- w_key: bfloat16 [4096, 512], P(None, 'mlp'), may hold values from -0.09375 to 0.09375
- w_value: bfloat16 [4096, 512], P(None, 'mlp'), may hold values from -0.09375 to 0.09375
- w_out: bfloat16 [2048, 4096], P('mlp'), may hold values from -0.125 to 0.125
- mlp_gain: bfloat16 [4096], replicated, may hold values from 0.5 to 1.5
- w_gate: bfloat16 [4096, 14336], P('mlp', 'req'), may hold values from -0.09375 to 0.09375
- w_up: bfloat16 [4096, 14336], P('mlp', 'req'), may hold values from -0.09375 to 0.09375
- w_down: bfloat16 [14336, 4096], P('req', 'mlp'), may hold values from -0.046875 to 0.046875
- prefix_kv: bfloat16 [65536, 2, 512], P('req', None, 'mlp'), may hold values from -512 to 512
- suffix_lengths: int32 [32, 4], P('req'), may hold values from 1 to 125, as said below
- prefix_owner: int32 [8, 4], replicated, may hold values from 0 to 3, each once within a row
Outputs:
- hidden_out: bfloat16 [4096, 4096], P('req', 'mlp')
- suffix_kv: bfloat16 [4096, 2, 512], P('req', None, 'mlp')
Inputs may be any that keep to these rules, and one draw needn't show every extreme that they name: `suffix_lengths`: the lengths of one index of req sum to at most 128; in every draw some index sums to exactly 128. `prefix_owner`: each row is a permutation.
All inputs are finite; a program needn't handle non-finite values.
Results may differ from a plain program's by a relative error of at most 0.02.
The roundings to bfloat16 on the way count: a program that leaves them out, or rounds other values in their place, can miss the bound.
Values may be sent and summed in bfloat16 or wider, within the bound.
No kernel may reach another device: no remote copies, remote signals or barrier semaphores. Data moves between devices by JAX's collectives and lax.ppermute only.
A program may use at most 128 MiB of HBM per device.

v0:
```python
import math
import jax
import jax.numpy as jnp
from jax import lax
from jax.sharding import PartitionSpec as P

HEAD_DIM = 128
PREFIX = 8192
GSPAN = 4
rope_base = 500000.0
eps = 1e-05


def from_partner(value, axis, stride):
    mask = 2**stride
    pairs = [(source, source ^ mask) for source in range(lax.axis_size(axis))]
    return lax.ppermute(value, axis, pairs)


def rope(values, positions):
    half = values.shape[-1] // 2
    freq = rope_base ** (-jnp.arange(half, dtype=jnp.float32) * 2.0 / values.shape[-1])
    angle = positions.astype(jnp.float32)[:, None] * freq[None, :]
    cosine = jnp.cos(angle)[:, None, :]
    sine = jnp.sin(angle)[:, None, :]
    former = values[..., :half]
    latter = values[..., half:]
    return jnp.concatenate(
        [former * cosine - latter * sine, latter * cosine + former * sine], axis=-1
    )


def rms_norm(values, gain):
    return (
        values
        * lax.rsqrt(jnp.mean(values * values, axis=-1, keepdims=True) + eps)
        * gain.astype(jnp.float32)
    )


def slot_layout(lengths, slot_count):
    ends = jnp.cumsum(lengths)
    starts = ends - lengths
    slot_ids = jnp.arange(slot_count, dtype=jnp.int32)
    request_of = jnp.sum((slot_ids[:, None] >= ends[None, :]).astype(jnp.int32), axis=1)
    picks = (request_of[:, None] == jnp.arange(lengths.shape[0], dtype=jnp.int32)[None, :]).astype(
        jnp.int32
    )
    start_of = jnp.sum(picks * starts[None, :], axis=1)
    positions = PREFIX + slot_ids - start_of
    return (request_of, request_of < lengths.shape[0], positions)


def partial_attention(grouped_queries, key_block, value_block, allowed):
    scores = jnp.einsum(
        "qkgd,nkd->kgqn", grouped_queries, key_block, preferred_element_type=jnp.float32
    ) / math.sqrt(grouped_queries.shape[-1])
    if allowed is not None:
        scores = jnp.where(allowed[None, None], scores, -jnp.inf)
    peak = jnp.max(scores, axis=-1)
    weights = jnp.exp(scores - peak[..., None])
    weight_sum = jnp.sum(weights, axis=-1)
    summed = jnp.einsum(
        "kgqn,nkd->kgqd",
        weights.astype(jnp.bfloat16),
        value_block,
        preferred_element_type=jnp.float32,
    )
    return (summed, peak, weight_sum)


def combine_states(former, latter):
    peak = jnp.maximum(former[1], latter[1])
    scale_former = jnp.exp(former[1] - peak)
    scale_latter = jnp.exp(latter[1] - peak)
    summed = former[0] * scale_former[..., None] + latter[0] * scale_latter[..., None]
    return (summed, peak, former[2] * scale_former + latter[2] * scale_latter)


def shards(
    hidden_in,
    attn_gain,
    w_query,
    w_key,
    w_value,
    w_out,
    mlp_gain,
    w_gate,
    w_up,
    w_down,
    prefix_kv,
    suffix_lengths,
    prefix_owner,
):
    slots_here = hidden_in.shape[0]
    head_dim = HEAD_DIM
    kv_heads = w_key.shape[1] // head_dim
    q_heads = w_query.shape[1] // head_dim
    group = q_heads // kv_heads
    block_len = prefix_kv.shape[0]
    span_bits = GSPAN.bit_length() - 1
    width_part = w_gate.shape[0]
    unit_count = w_gate.shape[1]
    request_of, live, positions = slot_layout(suffix_lengths[0], slots_here)
    hidden_f = hidden_in.astype(jnp.float32)
    normed = rms_norm(hidden_f, attn_gain).astype(jnp.bfloat16)
    query_rows = rope(
        jnp.dot(normed, w_query, preferred_element_type=jnp.float32).reshape(
            slots_here, q_heads, head_dim
        ),
        positions,
    ).astype(jnp.bfloat16)
    key_rows = rope(
        jnp.dot(normed, w_key, preferred_element_type=jnp.float32).reshape(
            slots_here, kv_heads, head_dim
        ),
        positions,
    ).astype(jnp.bfloat16)
    value_rows = (
        jnp.dot(normed, w_value, preferred_element_type=jnp.float32)
        .astype(jnp.bfloat16)
        .reshape(slots_here, kv_heads, head_dim)
    )
    grouped_queries = query_rows.reshape(slots_here, kv_heads, group, head_dim)
    place = lax.axis_index("req") % GSPAN
    group_id = lax.axis_index("req") // GSPAN
    owners = lax.dynamic_index_in_dim(prefix_owner, group_id, 0, keepdims=False)
    quarter = jnp.sum(jnp.where(owners == place, jnp.arange(GSPAN, dtype=jnp.int32), 0))
    prefix_pos = quarter * block_len + jnp.arange(block_len, dtype=jnp.int32)
    stored_keys = rope(
        prefix_kv[:, 0].reshape(block_len, kv_heads, head_dim).astype(jnp.float32), prefix_pos
    ).astype(jnp.bfloat16)
    stored_values = prefix_kv[:, 1].reshape(block_len, kv_heads, head_dim)
    blocks = jnp.stack([stored_keys, stored_values], axis=0)
    for bit_pos in range(span_bits):
        remote = from_partner(blocks, "req", bit_pos)
        blocks = jnp.concatenate([blocks, remote], axis=1)
    prefix_state = partial_attention(grouped_queries, blocks[0], blocks[1], None)
    slot_ids = jnp.arange(slots_here, dtype=jnp.int32)
    allowed = (request_of[:, None] == request_of[None, :]) & (
        slot_ids[None, :] <= slot_ids[:, None]
    )
    suffix_state = partial_attention(grouped_queries, key_rows, value_rows, allowed)
    merged, peak, weight_sum = combine_states(prefix_state, suffix_state)
    attended = (
        jnp.transpose(merged / weight_sum[..., None], (2, 0, 1, 3))
        .reshape(slots_here, q_heads * head_dim)
        .astype(jnp.bfloat16)
    )
    head_terms = jnp.dot(attended, w_out, preferred_element_type=jnp.float32)
    head_total = lax.psum(head_terms, "mlp")
    residual = (hidden_f + head_total).astype(jnp.bfloat16)
    normed_mlp = rms_norm(residual.astype(jnp.float32), mlp_gain).astype(jnp.bfloat16)
    width_start = lax.axis_index("mlp") * width_part
    normed_part = lax.dynamic_slice_in_dim(normed_mlp, width_start, width_part, 1)
    both_weights = jnp.concatenate([w_gate, w_up], axis=1)
    partial_sums = jnp.dot(
        lax.all_gather(normed_part, "req", axis=0, tiled=True),
        both_weights,
        preferred_element_type=jnp.float32,
    )
    gate_up = lax.psum(partial_sums, "mlp")
    act = (jax.nn.silu(gate_up[:, :unit_count]) * gate_up[:, unit_count:]).astype(jnp.bfloat16)
    down = lax.psum_scatter(
        jnp.dot(act, w_down, preferred_element_type=jnp.float32).astype(jnp.bfloat16),
        "req",
        scatter_dimension=0,
        tiled=True,
    ).astype(jnp.float32)
    residual_part = lax.dynamic_slice_in_dim(residual, width_start, width_part, 1).astype(
        jnp.float32
    )
    hidden_out = jnp.where(live[:, None], residual_part + down, 0.0).astype(jnp.bfloat16)
    stacked_kv = jnp.stack(
        [
            key_rows.reshape(slots_here, kv_heads * head_dim),
            value_rows.reshape(slots_here, kv_heads * head_dim),
        ],
        axis=1,
    )
    suffix_kv = jnp.where(live[:, None, None], stacked_kv, jnp.zeros_like(stacked_kv))
    return (hidden_out, suffix_kv)


def solution(mesh):
    placed = (
        P("req", None),
        P(),
        P(None, "mlp"),
        P(None, "mlp"),
        P(None, "mlp"),
        P("mlp", None),
        P(),
        P("mlp", "req"),
        P("mlp", "req"),
        P("req", "mlp"),
        P("req", None, "mlp"),
        P("req", None),
        P(),
    )
    return jax.shard_map(
        shards,
        mesh=mesh,
        in_specs=placed,
        out_specs=(P("req", "mlp"), P("req", None, "mlp")),
        check_vma=False,
    )
```

profile of v0, /device:TPU:0, one launch (start us, length us, event | category | flops | bytes accessed | tf_op | source)
XLA Modules:
  0.0 613.3 jit_solution(10236745792863355686)
XLA Ops:
  7.2 0.0 all-reduce.3.cloned.1.call-start
  7.3 0.9 fusion.62
  8.2 0.6 select_reduce_fusion.1
  9.5 3.3 fusion.76
  12.9 0.1 copy_convert_fusion
  13.0 0.1 copy.52
  13.0 4.8 fusion.42
  17.9 1.3 pad_maximum_fusion.2
  19.2 0.2 reduce-window.4
  19.4 0.1 convert_reduce_fusion
  19.4 0.1 select_reduce_fusion
  19.5 1.5 fusion.8
  21.1 3.3 fusion.71
  24.4 2.9 pad_maximum_fusion.1
  27.2 2.0 collective-permute-start.1
  29.3 0.1 reshape.468
  29.4 0.1 fusion.48
  29.5 1.9 convolution_bitcast_fusion
  31.4 0.2 fusion.54
  31.6 0.3 multiply_cosine_fusion.1
  32.0 0.2 fusion.77
  32.2 0.1 subtract_convert_fusion
  32.2 0.3 fusion.78
  32.5 0.1 fusion.43
  32.6 1.9 convolution_convert_fusion.1
  34.5 41.4 %collective-permute-done.1 = bf16[2,4096,1,128]{3,1,2,0:T(8,128)(2,1)} collective-permute-done((bf16[2,4096,1,128]{3,1,2,0:T(8,128)(2,1)}, bf16[2,4096,1,128]{3,1,2,0:T(8,128)(2,1)}, u32[]{:S(2)}, u32[]{:S(2)}) %collective-permute-start.1) | collective-permute-done | bytes 2097184 | tf_op jit(solution)/shard_map/ppermute | solution.py:17
  75.9 5.6 pad_maximum_fusion
  81.5 8.1 %bitcast_reduce_fusion = (f32[4,128]{1,0:T(4,128)S(1)}, f32[8192,128,4]{1,0,2:T(8,128)}) fusion(bf16[128,4,64]{2,0,1:T(8,128)(2,1)S(1)} %get-tuple-element.16, bf16[128,4,64]{2,0,1:T(8,128)(2,1)S(1)} %get-tuple-element.15, bf16[2,8192,1,128]{3,1,2,0:T(8,128)(2,1)S(1)} %pad_maximum_fusion), kind=kOutput, calls=%fused_computation.1 | convolution fusion | flops 1082392064 | bytes 19138560 | tf_op jit(solution)/shard_map/qkgd,nkd->kgqn/dot_general | solution.py:55
  89.6 8.5 %fusion.1 = f32[4,128]{1,0:T(4,128)S(1)} fusion(f32[8192,128,4]{1,0,2:T(8,128)} %get-tuple-element.26, f32[4,128]{1,0:T(4,128)S(1)} %get-tuple-element.25), kind=kLoop, calls=%fused_computation.3 | loop fusion | flops 12582400 | bytes 16781312 | tf_op jit(solution)/shard_map/reduce_sum | solution.py:62
  98.1 0.2 convolution_multiply_fusion
  98.4 7.6 %fusion.32 = bf16[4,128,128]{1,2,0:T(8,128)(2,1)S(1)} fusion(f32[4,128,128]{1,2,0:T(8,128)S(1)} %convolution_multiply_fusion, bf16[2,8192,1,128]{3,1,2,0:T(8,128)(2,1)S(1)} %pad_maximum_fusion, f32[8192,128,4]{1,0,2:T(8,128)} %get-tuple-element.26, f32[4,128]{1,0:T(4,128)S(1)} %get-tuple-element.25, f32[4,128]{1,0:T(4,128)S(1)} %get-tuple-element.8, ...), kind=kOutput, calls=%fused_computation.42 | convolution fusion | flops 1086586880 | bytes 19273728 | tf_op jit(solution)/shard_map/kgqn,nkd->kgqd/dot_general | solution.py:63
  106.0 2.0 fusion.79
  108.0 0.0 all-reduce.3.cloned.1.call-update
  108.1 0.0 all-gather.2.cloned.1.call-start
  108.2 60.9 %all-reduce.3.cloned.1.call-done = f32[128,4096]{1,0:T(8,128)} async-done(((f32[128,4096]{1,0:T(8,128)}), f32[128,4096]{1,0:T(8,128)}) %all-reduce.3.cloned.1.call-update) | async-done | bytes 2097168 | tf_op jit(solution)/shard_map/psum | solution.py:151
  169.1 2.0 multiply_reduce_fusion
  171.1 0.2 convert_element_type.119
  171.3 0.8 fusion.40
  172.2 0.0 all-gather.2.cloned.1.call-update
  172.2 0.0 all-reduce.5.cloned.1.call-start
  172.2 52.7 %all-gather.2.cloned.1.call-done = bf16[4096,1024]{1,0:T(8,128)(2,1)} async-done(((bf16[128,1024]{1,0:T(8,128)(2,1)}), bf16[4096,1024]{1,0:T(8,128)(2,1)}) %all-gather.2.cloned.1.call-update) | async-done | bytes 8388624 | tf_op jit(solution)/shard_map/all_gather | solution.py:158
  225.0 14.6 %fusion.13 = f32[4096,896]{1,0:T(8,128)} fusion(bf16[4096,1024]{1,0:T(8,128)(2,1)} %all-gather.2.cloned.1.call-done, bf16[1024,448]{0,1:T(8,128)(2,1)S(1)} %copy-done.9, bf16[1024,448]{0,1:T(8,128)(2,1)} %param.20), kind=kOutput, calls=%fused_computation.23 | convolution fusion | flops 7519862784 | bytes 24903680 | tf_op jit(solution)/shard_map/dot_general | solution.py:157
  239.6 0.0 reduce-scatter.2.cloned.1.call-start
  239.6 261.4 %all-reduce.5.cloned.1.call-done = f32[4096,896]{1,0:T(8,128)} async-done(((f32[4096,896]{1,0:T(8,128)}), f32[4096,896]{1,0:T(8,128)}) %all-reduce.5.cloned.1.call-update) | async-done | bytes 14680080 | tf_op jit(solution)/shard_map/psum | solution.py:162
  501.1 10.8 %convolution_convert_fusion = bf16[4096,1024]{1,0:T(8,128)(2,1)} fusion(bf16[448,1024]{1,0:T(8,128)(2,1)S(1)} %copy-done.10, f32[4096,896]{1,0:T(8,128)} %all-reduce.5.cloned.1.call-done), kind=kOutput, calls=%fused_computation.9 | convolution fusion | flops 3773300736 | bytes 26083328 | tf_op jit(solution)/shard_map/dot_general | solution.py:165
  512.0 0.8 copy.34
  512.7 92.2 %reduce-scatter.2.cloned.1.call-done = bf16[128,1024]{1,0:T(8,128)(2,1)} async-done(((bf16[4096,1024]{1,0:T(8,128)(2,1)}), bf16[128,1024]{1,0:T(8,128)(2,1)}) %reduce-scatter.2.cloned.1.call-update) | async-done | bytes 262160 | tf_op jit(solution)/shard_map/reduce_scatter | solution.py:164
  605.0 1.7 select_convert_fusion
  (39 shorter events, 0.2 us)
Async XLA Ops:
  7.2 22.3 %copy-start = (bf16[4096,128]{1,0:T(8,128)(2,1)S(1)}, bf16[4096,128]{1,0:T(8,128)(2,1)}, u32[]{:S(2)}) copy-start(bf16[4096,128]{1,0:T(8,128)(2,1)} %param.16) | copy-start | bytes 3145732
  7.2 161.9 %all-reduce.3.cloned.1.call-start = ((), (), s32[]{:S(2)}) async-start(), calls=%async_computation.1 | async-start | bytes 4194304 | tf_op jit(solution)/shard_map/psum | solution.py:151
  12.9 6.2 %copy-start.11 = (s32[1,4]{1,0:T(1,128)S(1)}, s32[1,4]{1,0:T(1,128)}, u32[]{:S(2)}) copy-start(s32[1,4]{1,0:T(1,128)} %param.24) | copy-start | bytes 52
  12.9 6.4 %copy-start.6 = (bf16[4096]{0:T(1024)(128)(2,1)S(1)}, bf16[4096]{0:T(1024)(128)(2,1)}, u32[]{:S(2)}) copy-start(bf16[4096]{0:T(1024)(128)(2,1)} %param.14) | copy-start | bytes 24580
  17.9 6.5 %copy-start.2 = (bf16[1,2048,1,64]{3,1,2,0:T(8,128)(2,1)}, bf16[1,2048,1,64]{3,1,2,0:T(8,128)(2,1)S(1)}, u32[]{:S(2)}) copy-start(bf16[1,2048,1,64]{3,1,2,0:T(8,128)(2,1)S(1)} %get-tuple-element.12) | copy-start | bytes 786436
  19.2 5.2 collective-permute-start
  27.2 48.6 %collective-permute-start.1 = (bf16[2,4096,1,128]{3,1,2,0:T(8,128)(2,1)}, bf16[2,4096,1,128]{3,1,2,0:T(8,128)(2,1)}, u32[]{:S(2)}, u32[]{:S(2)}) collective-permute-start(bf16[2,4096,1,128]{3,1,2,0:T(8,128)(2,1)} %pad_maximum_fusion.1), channel_id=1, source_target_pairs={{0,8},{4,12},{8,0},{12,4},{16,24},{20,28},{24,16},{28,20},{32,40},... | collective-permute-start | bytes 6291464 | tf_op jit(solution)/shard_map/ppermute | solution.py:17
  29.4 3.2 copy-start.8
  29.4 46.5 %copy-start.3 = (bf16[1,2048,1,64]{3,1,2,0:T(8,128)(2,1)S(1)}, bf16[1,2048,1,64]{3,1,2,0:T(8,128)(2,1)}, u32[]{:S(2)}) copy-start(bf16[1,2048,1,64]{3,1,2,0:T(8,128)(2,1)} %copy-done.2) | copy-start | bytes 786436
  98.3 7.6 %copy-start.5 = (bf16[512,4096]{1,0:T(8,128)(2,1)S(1)}, bf16[512,4096]{1,0:T(8,128)(2,1)}, u32[]{:S(2)}) copy-start(bf16[512,4096]{1,0:T(8,128)(2,1)} %param.18) | copy-start | bytes 12582916
  106.0 2.1 copy-start.7
  106.0 63.1 %copy-start.4 = (bf16[128,4096]{1,0:T(8,128)(2,1)S(1)}, bf16[128,4096]{1,0:T(8,128)(2,1)}, u32[]{:S(2)}) copy-start(bf16[128,4096]{1,0:T(8,128)(2,1)} %param.13) | copy-start | bytes 3145732
  108.1 116.9 %all-gather.2.cloned.1.call-start = ((), (), s32[]{:S(2)}) async-start(), calls=%async_computation.2 | async-start | bytes 8650752 | tf_op jit(solution)/shard_map/all_gather | solution.py:158
  108.1 116.8 %copy-start.9 = (bf16[1024,448]{0,1:T(8,128)(2,1)S(1)}, bf16[1024,448]{0,1:T(8,128)(2,1)}, u32[]{:S(2)}) copy-start(bf16[1024,448]{0,1:T(8,128)(2,1)} %param.21) | copy-start | bytes 2752516
  172.2 328.9 %all-reduce.5.cloned.1.call-start = ((), (), s32[]{:S(2)}) async-start(), calls=%async_computation.3 | async-start | bytes 29360128 | tf_op jit(solution)/shard_map/psum | solution.py:162
  239.6 261.5 %copy-start.10 = (bf16[448,1024]{1,0:T(8,128)(2,1)S(1)}, bf16[448,1024]{1,0:T(8,128)(2,1)}, u32[]{:S(2)}) copy-start(bf16[448,1024]{1,0:T(8,128)(2,1)} %param.22) | copy-start | bytes 2752516
  239.6 365.4 %reduce-scatter.2.cloned.1.call-start = ((), (), s32[]{:S(2)}) async-start(), calls=%async_computation.4 | async-start | bytes 8650752 | tf_op jit(solution)/shard_map/reduce_scatter | solution.py:164
  511.9 94.8 %copy-start.1 = (bf16[4096,128]{1,0:T(8,128)(2,1)S(1)}, bf16[4096,128]{1,0:T(8,128)(2,1)}, u32[]{:S(2)}) copy-start(bf16[4096,128]{1,0:T(8,128)(2,1)} %param.16) | copy-start | bytes 3145732
Sparse Core Ops, SparseCore 0:
  108.2 60.8 all-reduce.2
  172.3 52.6 all-gather.1
  239.7 261.3 all-reduce.4
  512.1 92.8 reduce-scatter.1
where the time goes:
time: 614 us; the launch traced here: 613 us
  waiting for transfers between devices  509 us (83%)
  matrix products  50.8 us (8%)
  other arithmetic  32.2 us (5%)
  between operations  14.8 us (2%)
    psum x1, waiting for transfers between devices, shards(): gate_up = lax.psum(partial_sums, 'mlp')  261 us
    reduce_scatter x1, waiting for transfers between devices, shards(): lax.psum_scatter(jnp.dot(act, w_down, preferred_element_type=jnp.float32)...  92.2 us
    psum x1, waiting for transfers between devices, shards(): head_total = lax.psum(head_terms, 'mlp')  60.9 us
    all_gather x1, waiting for transfers between devices, shards(): lax.all_gather(normed_part, 'req', axis=0, tiled=True)  52.7 us
    ppermute x2, waiting for transfers between devices, from_partner(): return lax.ppermute(value, axis, pairs)  41.4 us
    dot_general x1, matrix products, shards(): jnp.dot(lax.all_gather(normed_part, 'req', axis=0, tiled=True), both_weig...  14.6 us
  transfers between devices with their start and end apart: 6, of which 5 were waited for; matrix products, arithmetic and copies ran while one was open for 2% of the time, Pallas kernels for 0%

commit v1 on v0

--- a/solution.py
+++ b/solution.py
@@ -155,7 +155,9 @@
     normed_part = lax.dynamic_slice_in_dim(normed_mlp, width_start, width_part, 1)
     both_weights = jnp.concatenate([w_gate, w_up], axis=1)
     partial_sums = jnp.dot(
-        lax.all_gather(normed_part, "req", axis=0, tiled=True),
+        jnp.concatenate(
+            lax.all_to_all(jnp.stack([normed_part] * lax.axis_size("req")), "req", 0, 0), axis=0
+        ),
         both_weights,
         preferred_element_type=jnp.float32,
     )

time: 614 us -> 658 us (1.072)
  blocking collectives: 0 us -> 103 us
  waiting for transfers between devices: 509 us -> 453 us
    all_to_all x0 -> x1, blocking collectives: none -> 103 us  [shards(): lax.all_to_all(jnp.stack([normed_part] * lax.axis_size('req')), 'req', 0, 0)]
    all_gather x1 -> x0, waiting for transfers between devices: 52.7 us -> none  [shards(): lax.all_gather(normed_part, 'req', axis=0, tiled=True)]
  transfers between devices with their start and end apart: 6 -> 5, of which waited for: 5 -> 4; matrix products, arithmetic and copies ran while one was open for 2% -> 2% of each run, Pallas kernels for 0% -> 0%
where the time goes in v1:
time: 658 us
  waiting for transfers between devices  453 us (69%)
  blocking collectives  103 us (16%)
  matrix products  47.7 us (7%)
  other arithmetic  31.5 us (5%)
  between operations  14.8 us (2%)
    psum x1, waiting for transfers between devices, shards(): gate_up = lax.psum(partial_sums, 'mlp')  259 us
    all_to_all x1, blocking collectives, shards(): lax.all_to_all(jnp.stack([normed_part] * lax.axis_size('req')), 'req', 0, 0)  103 us
    reduce_scatter x1, waiting for transfers between devices, shards(): lax.psum_scatter(jnp.dot(act, w_down, preferred_element_type=jnp.float32)...  92.2 us
    psum x1, waiting for transfers between devices, shards(): head_total = lax.psum(head_terms, 'mlp')  61 us
    ppermute x2, waiting for transfers between devices, from_partner(): return lax.ppermute(value, axis, pairs)  41.4 us
  transfers between devices with their start and end apart: 5, of which 4 were waited for; matrix products, arithmetic and copies ran while one was open for 2% of the time, Pallas kernels for 0%

profile of v1, /device:TPU:0, one launch (start us, length us, event | category | flops | bytes accessed | tf_op | source)
XLA Modules:
  0.0 657.5 jit_solution(9798923859189480040)
XLA Ops:
  7.2 0.0 all-reduce.3.cloned.1.call-start
  7.3 0.9 fusion.62
  8.2 0.6 select_reduce_fusion.1
  9.5 3.3 fusion.76
  12.9 0.1 copy_convert_fusion
  13.0 0.1 copy.52
  13.0 4.8 fusion.42
  17.9 1.3 pad_maximum_fusion.2
  19.2 0.2 reduce-window.4
  19.4 0.1 convert_reduce_fusion
  19.4 0.1 select_reduce_fusion
  19.5 1.5 fusion.8
  21.1 3.3 fusion.71
  24.4 2.9 pad_maximum_fusion.1
  27.2 2.0 collective-permute-start.1
  29.3 0.1 reshape.473
  29.4 0.1 fusion.48
  29.5 1.9 convolution_bitcast_fusion
  31.4 0.2 fusion.54
  31.6 0.3 multiply_cosine_fusion.1
  32.0 0.2 fusion.77
  32.2 0.1 subtract_convert_fusion
  32.2 0.3 fusion.78
  32.5 0.1 fusion.43
  32.6 1.9 convolution_convert_fusion.1
  34.5 41.4 %collective-permute-done.1 = bf16[2,4096,1,128]{3,1,2,0:T(8,128)(2,1)} collective-permute-done((bf16[2,4096,1,128]{3,1,2,0:T(8,128)(2,1)}, bf16[2,4096,1,128]{3,1,2,0:T(8,128)(2,1)}, u32[]{:S(2)}, u32[]{:S(2)}) %collective-permute-start.1) | collective-permute-done | bytes 2097184 | tf_op jit(solution)/shard_map/ppermute | solution.py:17
  75.9 5.6 pad_maximum_fusion
  81.5 8.1 %bitcast_reduce_fusion = (f32[4,128]{1,0:T(4,128)S(1)}, f32[8192,128,4]{1,0,2:T(8,128)}) fusion(bf16[128,4,64]{2,0,1:T(8,128)(2,1)S(1)} %get-tuple-element.16, bf16[128,4,64]{2,0,1:T(8,128)(2,1)S(1)} %get-tuple-element.15, bf16[2,8192,1,128]{3,1,2,0:T(8,128)(2,1)S(1)} %pad_maximum_fusion), kind=kOutput, calls=%fused_computation.1 | convolution fusion | flops 1082392064 | bytes 19138560 | tf_op jit(solution)/shard_map/qkgd,nkd->kgqn/dot_general | solution.py:55
  89.6 8.5 %fusion.1 = f32[4,128]{1,0:T(4,128)S(1)} fusion(f32[8192,128,4]{1,0,2:T(8,128)} %get-tuple-element.26, f32[4,128]{1,0:T(4,128)S(1)} %get-tuple-element.25), kind=kLoop, calls=%fused_computation.3 | loop fusion | flops 12582400 | bytes 16781312 | tf_op jit(solution)/shard_map/reduce_sum | solution.py:62
  98.1 0.2 convolution_multiply_fusion
  98.4 7.6 %fusion.32 = bf16[4,128,128]{1,2,0:T(8,128)(2,1)S(1)} fusion(f32[4,128,128]{1,2,0:T(8,128)S(1)} %convolution_multiply_fusion, bf16[2,8192,1,128]{3,1,2,0:T(8,128)(2,1)S(1)} %pad_maximum_fusion, f32[8192,128,4]{1,0,2:T(8,128)} %get-tuple-element.26, f32[4,128]{1,0:T(4,128)S(1)} %get-tuple-element.25, f32[4,128]{1,0:T(4,128)S(1)} %get-tuple-element.8, ...), kind=kOutput, calls=%fused_computation.42 | convolution fusion | flops 1086586880 | bytes 19273728 | tf_op jit(solution)/shard_map/kgqn,nkd->kgqd/dot_general | solution.py:63
  106.0 2.0 fusion.79
  108.0 0.0 all-reduce.3.cloned.1.call-update
  108.1 0.0 all-reduce.5.cloned.1.call-start
  108.1 61.0 %all-reduce.3.cloned.1.call-done = f32[128,4096]{1,0:T(8,128)} async-done(((f32[128,4096]{1,0:T(8,128)}), f32[128,4096]{1,0:T(8,128)}) %all-reduce.3.cloned.1.call-update) | async-done | bytes 2097168 | tf_op jit(solution)/shard_map/psum | solution.py:151
  169.1 2.0 multiply_reduce_fusion
  171.1 0.2 convert_element_type.119
  171.3 0.1 fusion.40
  171.5 1.1 stack.7
  172.5 102.6 %all_to_all.5 = bf16[32,128,1024]{2,1,0:T(8,128)(2,1)S(1)} all-to-all(bf16[32,128,1024]{2,1,0:T(8,128)(2,1)S(1)} %stack.7), channel_id=1, replica_groups=mesh['req'=32,'mlp'=4] {'req'}, dimensions={0} | all-to-all | bytes 16777216 | tf_op jit(solution)/shard_map/all_to_all | solution.py:159
  275.1 11.6 %fusion.13 = f32[4096,896]{1,0:T(8,128)} fusion(bf16[4096,1024]{1,0:T(8,128)(2,1)S(1)} %bitcast.106, bf16[1024,448]{0,1:T(8,128)(2,1)S(1)} %copy-done.9, bf16[1024,448]{0,1:T(8,128)(2,1)S(1)} %copy-done.10), kind=kOutput, calls=%fused_computation.23 | convolution fusion | flops 7519862784 | bytes 24903680 | tf_op jit(solution)/shard_map/dot_general | solution.py:157
  286.7 0.0 all-reduce.5.cloned.1.call-update
  286.8 0.0 reduce-scatter.2.cloned.1.call-start
  286.8 258.5 %all-reduce.5.cloned.1.call-done = f32[4096,896]{1,0:T(8,128)} async-done(((f32[4096,896]{1,0:T(8,128)}), f32[4096,896]{1,0:T(8,128)}) %all-reduce.5.cloned.1.call-update) | async-done | bytes 14680080 | tf_op jit(solution)/shard_map/psum | solution.py:164
  545.4 10.8 %convolution_convert_fusion = bf16[4096,1024]{1,0:T(8,128)(2,1)} fusion(bf16[448,1024]{1,0:T(8,128)(2,1)S(1)} %copy-done.11, f32[4096,896]{1,0:T(8,128)} %all-reduce.5.cloned.1.call-done), kind=kOutput, calls=%fused_computation.9 | convolution fusion | flops 3773300736 | bytes 26083328 | tf_op jit(solution)/shard_map/dot_general | solution.py:167
  556.3 0.8 copy.34
  557.0 92.2 %reduce-scatter.2.cloned.1.call-done = bf16[128,1024]{1,0:T(8,128)(2,1)} async-done(((bf16[4096,1024]{1,0:T(8,128)(2,1)}), bf16[128,1024]{1,0:T(8,128)(2,1)}) %reduce-scatter.2.cloned.1.call-update) | async-done | bytes 262160 | tf_op jit(solution)/shard_map/reduce_scatter | solution.py:166
  649.2 1.7 select_convert_fusion
  (40 shorter events, 0.2 us)
Async XLA Ops:
  7.2 22.3 %copy-start = (bf16[4096,128]{1,0:T(8,128)(2,1)S(1)}, bf16[4096,128]{1,0:T(8,128)(2,1)}, u32[]{:S(2)}) copy-start(bf16[4096,128]{1,0:T(8,128)(2,1)} %param.16) | copy-start | bytes 3145732
  7.2 161.9 %all-reduce.3.cloned.1.call-start = ((), (), s32[]{:S(2)}) async-start(), calls=%async_computation.2 | async-start | bytes 4194304 | tf_op jit(solution)/shard_map/psum | solution.py:151
  12.9 6.2 copy-start.12
  12.9 6.4 copy-start.6
  17.9 6.5 copy-start.2
  19.2 5.2 collective-permute-start
  27.2 48.6 %collective-permute-start.1 = (bf16[2,4096,1,128]{3,1,2,0:T(8,128)(2,1)}, bf16[2,4096,1,128]{3,1,2,0:T(8,128)(2,1)}, u32[]{:S(2)}, u32[]{:S(2)}) collective-permute-start(bf16[2,4096,1,128]{3,1,2,0:T(8,128)(2,1)} %pad_maximum_fusion.1), channel_id=1, source_target_pairs={{0,8},{4,12},{8,0},{12,4},{16,24},{20,28},{24,16},{28,20},{32,40},... | collective-permute-start | bytes 6291464 | tf_op jit(solution)/shard_map/ppermute | solution.py:17
  29.4 3.2 copy-start.8
  29.4 46.5 %copy-start.3 = (bf16[1,2048,1,64]{3,1,2,0:T(8,128)(2,1)S(1)}, bf16[1,2048,1,64]{3,1,2,0:T(8,128)(2,1)}, u32[]{:S(2)}) copy-start(bf16[1,2048,1,64]{3,1,2,0:T(8,128)(2,1)} %copy-done.2) | copy-start | bytes 786436
  98.3 7.6 %copy-start.5 = (bf16[512,4096]{1,0:T(8,128)(2,1)S(1)}, bf16[512,4096]{1,0:T(8,128)(2,1)}, u32[]{:S(2)}) copy-start(bf16[512,4096]{1,0:T(8,128)(2,1)} %param.18) | copy-start | bytes 12582916
  106.0 2.1 copy-start.7
  106.0 63.1 %copy-start.4 = (bf16[128,4096]{1,0:T(8,128)(2,1)S(1)}, bf16[128,4096]{1,0:T(8,128)(2,1)}, u32[]{:S(2)}) copy-start(bf16[128,4096]{1,0:T(8,128)(2,1)} %param.13) | copy-start | bytes 3145732
  108.1 437.3 %all-reduce.5.cloned.1.call-start = ((), (), s32[]{:S(2)}) async-start(), calls=%async_computation.3 | async-start | bytes 29360128 | tf_op jit(solution)/shard_map/psum | solution.py:164
  172.5 102.6 %copy-start.9 = (bf16[1024,448]{0,1:T(8,128)(2,1)S(1)}, bf16[1024,448]{0,1:T(8,128)(2,1)}, u32[]{:S(2)}) copy-start(bf16[1024,448]{0,1:T(8,128)(2,1)} %param.21) | copy-start | bytes 2752516
  172.5 102.6 %copy-start.10 = (bf16[1024,448]{0,1:T(8,128)(2,1)S(1)}, bf16[1024,448]{0,1:T(8,128)(2,1)}, u32[]{:S(2)}) copy-start(bf16[1024,448]{0,1:T(8,128)(2,1)} %param.20) | copy-start | bytes 2752516
  286.7 258.6 %copy-start.11 = (bf16[448,1024]{1,0:T(8,128)(2,1)S(1)}, bf16[448,1024]{1,0:T(8,128)(2,1)}, u32[]{:S(2)}) copy-start(bf16[448,1024]{1,0:T(8,128)(2,1)} %param.22) | copy-start | bytes 2752516
  286.8 362.5 %reduce-scatter.2.cloned.1.call-start = ((), (), s32[]{:S(2)}) async-start(), calls=%async_computation.4 | async-start | bytes 8650752 | tf_op jit(solution)/shard_map/reduce_scatter | solution.py:166
  556.2 94.8 %copy-start.1 = (bf16[4096,128]{1,0:T(8,128)(2,1)S(1)}, bf16[4096,128]{1,0:T(8,128)(2,1)}, u32[]{:S(2)}) copy-start(bf16[4096,128]{1,0:T(8,128)(2,1)} %param.16) | copy-start | bytes 3145732
Sparse Core Ops, SparseCore 0:
  108.2 60.8 all-reduce.2
  286.9 258.4 all-reduce.4
  556.3 92.8 reduce-scatter.1
